TPU v7x, 256 devices: a whole 4x4x8 slice. The times are simulated.
256 devices in a mesh: seq: 128 (over x, y, z_lo, core), dp: 2 (over z_hi).
Axes of the slice: x: 4, y: 4, z: 8 (z_hi: 2, z_lo: 4; z = z_hi * 4 + z_lo), core: 2. Of those that a mesh axis runs over, the one named last changes fastest.
Arguments:
- inputs: bfloat16 [2, 256, 256, 512], P('dp', 'seq'), may hold values from -6 to 6
- gate: bfloat16 [2, 256, 256, 512], P('dp', 'seq'), may hold values from -6 to 6
- kernel: bfloat16 [256, 256, 512], P(None, 'seq'), may hold values from -6 to 6
- first_blocks: bfloat16 [256, 256, 256], P('seq'), may hold values from -0.375 to 0.375
- second_blocks: bfloat16 [256, 256, 256], P('seq'), may hold values from -0.375 to 0.375
- cotangent: bfloat16 [2, 256, 256, 512], P('dp', 'seq'), may hold values from -6 to 6
Outputs:
- mixed: bfloat16 [2, 256, 256, 512], P('dp', 'seq')
- grad_inputs: bfloat16 [2, 256, 256, 512], P('dp', 'seq')
- grad_gate: bfloat16 [2, 256, 256, 512], P('dp', 'seq')
- grad_kernel: float32 [256, 256, 512], P(None, 'seq')
All inputs are finite; a program needn't handle non-finite values.
Results may differ from a plain program's by a relative error of at most 0.007.
Values may be sent and summed in bfloat16 or wider, within the bound.
No kernel may reach another device: no remote copies, remote signals or barrier semaphores. Data moves between devices by JAX's collectives and lax.ppermute only.
A program may use at most 64 MiB of HBM per device.

v0:
```python
import jax
import jax.numpy as jnp
from jax import lax
from jax.sharding import PartitionSpec as P


def shards(inputs, gate, kernel, first_blocks, second_blocks, cotangent):
    f32 = jnp.float32
    bf16 = jnp.bfloat16
    gate32 = gate.astype(f32)
    cot = cotangent.astype(f32)
    d_result = (cot * gate32).astype(bf16)

    def spread(rows):
        return jnp.einsum("rij,srjd->srid", first_blocks, rows, preferred_element_type=f32).astype(
            bf16
        )

    def mix_columns(piece):
        return jnp.einsum("cqr,srcd->sqcd", second_blocks, piece, preferred_element_type=f32)

    def unmix_columns(scaled):
        return jnp.einsum(
            "cqr,sqcd->srcd", second_blocks, scaled, preferred_element_type=f32
        ).astype(bf16)

    def finish_rows(piece):
        return jnp.einsum("rij,srid->srjd", first_blocks, piece, preferred_element_type=f32)

    second = mix_columns(
        lax.all_to_all(spread(inputs), "seq", split_axis=2, concat_axis=1, tiled=True)
    )
    hidden = (second * kernel).astype(bf16)
    result = finish_rows(
        lax.all_to_all(unmix_columns(hidden), "seq", split_axis=1, concat_axis=2, tiled=True)
    )
    d_hidden = mix_columns(
        lax.all_to_all(spread(d_result), "seq", split_axis=2, concat_axis=1, tiled=True)
    )
    d_second = (d_hidden * kernel).astype(bf16)
    d_inputs = finish_rows(
        lax.all_to_all(unmix_columns(d_second), "seq", split_axis=1, concat_axis=2, tiled=True)
    )
    mixed = (result * gate32).astype(bf16)
    grad_gate = (cot * result).astype(bf16)
    grad_inputs = d_inputs.astype(bf16)
    grad_kernel = lax.psum(jnp.sum(d_hidden * second, axis=0), "dp")
    return (mixed, grad_inputs, grad_gate, grad_kernel)


def solution(mesh):
    placed = (
        P("dp", "seq", None, None),
        P("dp", "seq", None, None),
        P(None, "seq", None),
        P("seq", None, None),
        P("seq", None, None),
        P("dp", "seq", None, None),
    )
    return jax.shard_map(
        shards,
        mesh=mesh,
        in_specs=placed,
        out_specs=(
            P("dp", "seq", None, None),
            P("dp", "seq", None, None),
            P("dp", "seq", None, None),
            P(None, "seq", None),
        ),
        check_vma=False,
    )
```

profile of v0, /device:TPU:1, one launch (start us, length us, event | category | flops | bytes accessed | tf_op | source)
XLA Modules:
  0.0 193.4 jit_solution(5639259495040109000)
XLA Ops:
  7.2 1.0 copy-done
  8.2 1.3 fusion
  9.5 1.2 copy.43
  10.7 14.0 %all-to-all-start = ((bf16[1,2,256,512]{3,1,0,2:T(2,128)(2,1)}), bf16[1,2,256,512]{3,1,0,2:T(2,128)(2,1)S(1)}, u32[]{:S(2)}, u32[]{:S(2)}) async-start(bf16[1,2,256,512]{3,1,0,2:T(2,128)(2,1)} %copy.43), calls=%async_computation | async-start | bytes 1048576 | tf_op jit(solution)/shard_map/all_to_all | solution.py:31
  24.9 0.8 copy-done.11
  25.9 0.7 copy-done.6
  27.0 0.4 copy-done.1
  27.5 1.2 copy.52
  28.6 14.2 %all-to-all-done = bf16[1,2,256,512]{3,1,0,2:T(2,128)(2,1)S(1)} async-done(((bf16[1,2,256,512]{3,1,0,2:T(2,128)(2,1)}), bf16[1,2,256,512]{3,1,0,2:T(2,128)(2,1)S(1)}, u32[]{:S(2)}, u32[]{:S(2)}) %all-to-all-start) | async-done | bytes 524320 | tf_op jit(solution)/shard_map/all_to_all | solution.py:31
  42.8 0.8 copy-done.8
  43.6 6.9 %all-to-all-start.2 = ((bf16[1,2,256,512]{3,1,0,2:T(2,128)(2,1)}), bf16[1,2,256,512]{3,1,0,2:T(2,128)(2,1)S(1)}, u32[]{:S(2)}, u32[]{:S(2)}) async-start(bf16[1,2,256,512]{3,1,0,2:T(2,128)(2,1)} %copy.52), calls=%async_computation.2 | async-start | bytes 1048576 | tf_op jit(solution)/shard_map/all_to_all | solution.py:38
  50.6 0.5 copy.46
  51.1 0.5 copy-done.9
  52.0 0.5 copy-done.5
  52.9 1.1 fusion.1
  54.0 2.0 %copy.47 = bf16[1,256,2,512]{3,2,0,1:T(2,128)(2,1)} copy(bf16[1,256,2,512]{1,3,2,0:T(8,128)(2,1)} %fusion.1) | data formatting | bytes 1048576 | tf_op jit(solution)/shard_map/convert_element_type | solution.py:25
  56.0 12.7 %all-to-all-done.2 = bf16[1,2,256,512]{3,1,0,2:T(2,128)(2,1)S(1)} async-done(((bf16[1,2,256,512]{3,1,0,2:T(2,128)(2,1)}), bf16[1,2,256,512]{3,1,0,2:T(2,128)(2,1)S(1)}, u32[]{:S(2)}, u32[]{:S(2)}) %all-to-all-start.2) | async-done | bytes 524320 | tf_op jit(solution)/shard_map/all_to_all | solution.py:38
  68.7 7.5 %all-to-all-start.1 = ((bf16[1,256,2,512]{3,2,0,1:T(2,128)(2,1)}), bf16[1,256,2,512]{3,2,0,1:T(2,128)(2,1)}, u32[]{:S(2)}, u32[]{:S(2)}) async-start(bf16[1,256,2,512]{3,2,0,1:T(2,128)(2,1)} %copy.47), calls=%async_computation.1 | async-start | bytes 1048576 | tf_op jit(solution)/shard_map/all_to_all | solution.py:35
  77.0 0.7 copy-done.4
  77.7 1.1 fusion.3
  78.8 2.0 %copy.55 = bf16[1,256,2,512]{3,2,0,1:T(2,128)(2,1)} copy(bf16[1,256,2,512]{1,3,2,0:T(8,128)(2,1)} %fusion.3) | data formatting | bytes 1048576 | tf_op jit(solution)/shard_map/convert_element_type | solution.py:25
  80.8 13.4 %all-to-all-done.1 = bf16[1,256,2,512]{3,2,0,1:T(2,128)(2,1)} async-done(((bf16[1,256,2,512]{3,2,0,1:T(2,128)(2,1)}), bf16[1,256,2,512]{3,2,0,1:T(2,128)(2,1)}, u32[]{:S(2)}, u32[]{:S(2)}) %all-to-all-start.1) | async-done | bytes 524320 | tf_op jit(solution)/shard_map/all_to_all | solution.py:35
  94.1 7.7 %all-to-all-start.3 = ((bf16[1,256,2,512]{3,2,0,1:T(2,128)(2,1)}), bf16[1,256,2,512]{3,2,0,1:T(2,128)(2,1)}, u32[]{:S(2)}, u32[]{:S(2)}) async-start(bf16[1,256,2,512]{3,2,0,1:T(2,128)(2,1)} %copy.55), calls=%async_computation.3 | async-start | bytes 1048576 | tf_op jit(solution)/shard_map/all_to_all | solution.py:42
  101.8 1.1 multiply_bitcast_fusion
  103.0 1.5 copy.48
  104.9 1.0 copy.58
  105.9 13.8 %all-to-all-done.3 = bf16[1,256,2,512]{3,2,0,1:T(2,128)(2,1)} async-done(((bf16[1,256,2,512]{3,2,0,1:T(2,128)(2,1)}), bf16[1,256,2,512]{3,2,0,1:T(2,128)(2,1)}, u32[]{:S(2)}, u32[]{:S(2)}) %all-to-all-start.3) | async-done | bytes 524320 | tf_op jit(solution)/shard_map/all_to_all | solution.py:42
  119.7 1.5 copy.56
  121.5 1.0 copy.59
  122.5 1.0 copy.60
  123.5 60.8 %all-reduce.2.cloned.1.call-done = f32[256,2,512]{0,2,1:T(8,128)} async-done(((f32[256,2,512]{0,2,1:T(8,128)}), f32[256,2,512]{0,2,1:T(8,128)}) %all-reduce.2.cloned.1.call-update) | async-done | bytes 1048592 | tf_op jit(solution)/shard_map/psum | solution.py:47
  184.3 2.2 %copy.61 = f32[256,2,512]{2,1,0:T(2,128)} copy(f32[256,2,512]{0,2,1:T(8,128)} %all-reduce.2.cloned.1.call-done) | data formatting | bytes 2097152
  (29 shorter events, 3.1 us)
Async XLA Ops:
  7.2 1.0 copy-start
  10.7 14.0 %copy-start.10 = (bf16[1,2,256,512]{3,2,1,0:T(8,128)(2,1)S(1)}, bf16[1,2,256,512]{3,2,1,0:T(8,128)(2,1)}, u32[]{:S(2)}) copy-start(bf16[1,2,256,512]{3,2,1,0:T(8,128)(2,1)} %param.11) | copy-start | bytes 1572868
  10.7 32.1 %all-to-all-start = ((bf16[1,2,256,512]{3,1,0,2:T(2,128)(2,1)}), bf16[1,2,256,512]{3,1,0,2:T(2,128)(2,1)S(1)}, u32[]{:S(2)}, u32[]{:S(2)}) async-start(bf16[1,2,256,512]{3,1,0,2:T(2,128)(2,1)} %copy.43), calls=%async_computation | async-start | bytes 1048576 | tf_op jit(solution)/shard_map/all_to_all | solution.py:31
  24.7 1.0 copy-start.11
  25.7 0.9 copy-start.6
  26.7 0.8 copy-start.1
  28.6 21.9 %copy-start.12 = (bf16[256,2,512]{2,1,0:T(2,128)(2,1)S(1)}, bf16[256,2,512]{2,1,0:T(2,128)(2,1)}, u32[]{:S(2)}) copy-start(bf16[256,2,512]{2,1,0:T(2,128)(2,1)} %param.8) | copy-start | bytes 1572868
  42.8 0.8 copy-start.8
  43.6 25.1 %all-to-all-start.2 = ((bf16[1,2,256,512]{3,1,0,2:T(2,128)(2,1)}), bf16[1,2,256,512]{3,1,0,2:T(2,128)(2,1)S(1)}, u32[]{:S(2)}, u32[]{:S(2)}) async-start(bf16[1,2,256,512]{3,1,0,2:T(2,128)(2,1)} %copy.52), calls=%async_computation.2 | async-start | bytes 1048576 | tf_op jit(solution)/shard_map/all_to_all | solution.py:38
  50.6 1.0 copy-start.9
  51.1 1.8 copy-start.3
  51.6 0.9 copy-start.5
  68.7 25.4 %all-to-all-start.1 = ((bf16[1,256,2,512]{3,2,0,1:T(2,128)(2,1)}), bf16[1,256,2,512]{3,2,0,1:T(2,128)(2,1)}, u32[]{:S(2)}, u32[]{:S(2)}) async-start(bf16[1,256,2,512]{3,2,0,1:T(2,128)(2,1)} %copy.47), calls=%async_computation.1 | async-start | bytes 1048576 | tf_op jit(solution)/shard_map/all_to_all | solution.py:35
  76.6 1.0 copy-start.4
  94.1 25.6 %all-to-all-start.3 = ((bf16[1,256,2,512]{3,2,0,1:T(2,128)(2,1)}), bf16[1,256,2,512]{3,2,0,1:T(2,128)(2,1)}, u32[]{:S(2)}, u32[]{:S(2)}) async-start(bf16[1,256,2,512]{3,2,0,1:T(2,128)(2,1)} %copy.55), calls=%async_computation.3 | async-start | bytes 1048576 | tf_op jit(solution)/shard_map/all_to_all | solution.py:42
  101.8 82.6 %all-reduce.2.cloned.1.call-start = ((), (), s32[]{:S(2)}) async-start(), calls=%async_computation.4 | async-start | bytes 2097152 | tf_op jit(solution)/shard_map/psum | solution.py:47
  103.0 1.6 copy-start.2
  103.0 1.6 copy-start.7
Sparse Core Ops, SparseCore 0:
  105.8 78.5 all-reduce.1
where the time goes:
time: 194 us; the launch traced here: 193 us
  waiting for transfers between devices  115 us (59%)
  starting transfers between devices  36.1 us (19%)
  local copies, waits for them, and re-layouts  21.9 us (11%)
  between operations  14.2 us (7%)
  matrix products  5.23 us (3%)
    psum x1, waiting for transfers between devices, shards(): grad_kernel = lax.psum(jnp.sum(d_hidden * second, axis=0), 'dp')  60.8 us
    all_to_all x1, waiting for transfers between devices, shards(): lax.all_to_all(spread(inputs), 'seq', split_axis=2, concat_axis=1, tiled=...  14.2 us
    all_to_all x1, starting transfers between devices, shards(): lax.all_to_all(spread(inputs), 'seq', split_axis=2, concat_axis=1, tiled=...  14 us
    all_to_all x1, waiting for transfers between devices, shards(): lax.all_to_all(unmix_columns(d_second), 'seq', split_axis=1, concat_axis=...  13.8 us
    all_to_all x1, waiting for transfers between devices, shards(): lax.all_to_all(unmix_columns(hidden), 'seq', split_axis=1, concat_axis=2,...  13.4 us
    all_to_all x1, waiting for transfers between devices, shards(): lax.all_to_all(spread(d_result), 'seq', split_axis=2, concat_axis=1, tile...  12.7 us
    unnamed x33, local copies, waits for them, and re-layouts  11.8 us
    all_to_all x1, starting transfers between devices, shards(): lax.all_to_all(unmix_columns(d_second), 'seq', split_axis=1, concat_axis=...  7.66 us
  transfers between devices with their start and end apart: 5, of which 5 were waited for; matrix products, arithmetic and copies ran while one was open for 9% of the time, Pallas kernels for 0%

commit v1 on v0

--- a/solution.py
+++ b/solution.py
@@ -7,6 +7,7 @@
 def shards(inputs, gate, kernel, first_blocks, second_blocks, cotangent):
     f32 = jnp.float32
     bf16 = jnp.bfloat16
+    seqs = inputs.shape[0]
     gate32 = gate.astype(f32)
     cot = cotangent.astype(f32)
     d_result = (cot * gate32).astype(bf16)
@@ -27,24 +28,24 @@
     def finish_rows(piece):
         return jnp.einsum("rij,srid->srjd", first_blocks, piece, preferred_element_type=f32)
 
-    second = mix_columns(
-        lax.all_to_all(spread(inputs), "seq", split_axis=2, concat_axis=1, tiled=True)
+    both = jnp.concatenate([inputs, d_result], axis=0)
+    mixed_both = mix_columns(
+        lax.all_to_all(spread(both), "seq", split_axis=2, concat_axis=1, tiled=True)
     )
-    hidden = (second * kernel).astype(bf16)
-    result = finish_rows(
-        lax.all_to_all(unmix_columns(hidden), "seq", split_axis=1, concat_axis=2, tiled=True)
+    second = mixed_both[:seqs]
+    d_hidden = mixed_both[seqs:]
+    partial = jnp.sum(d_hidden * second, axis=0)
+    other = lax.ppermute(partial, "dp", perm=[(0, 1), (1, 0)])
+    scaled = (mixed_both * kernel).astype(bf16)
+    out_both = finish_rows(
+        lax.all_to_all(unmix_columns(scaled), "seq", split_axis=1, concat_axis=2, tiled=True)
     )
-    d_hidden = mix_columns(
-        lax.all_to_all(spread(d_result), "seq", split_axis=2, concat_axis=1, tiled=True)
-    )
-    d_second = (d_hidden * kernel).astype(bf16)
-    d_inputs = finish_rows(
-        lax.all_to_all(unmix_columns(d_second), "seq", split_axis=1, concat_axis=2, tiled=True)
-    )
+    result = out_both[:seqs]
+    d_inputs = out_both[seqs:]
     mixed = (result * gate32).astype(bf16)
     grad_gate = (cot * result).astype(bf16)
     grad_inputs = d_inputs.astype(bf16)
-    grad_kernel = lax.psum(jnp.sum(d_hidden * second, axis=0), "dp")
+    grad_kernel = partial + other
     return (mixed, grad_inputs, grad_gate, grad_kernel)
 
 

time: 194 us -> 145 us (0.75)
  waiting for transfers between devices: 115 us -> 94.2 us
  between operations: 14.2 us -> 0.79 us
  starting transfers between devices: 36.1 us -> 25.6 us
  local copies, waits for them, and re-layouts: 21.9 us -> 18.8 us
  matrix products: 5.23 us -> 3.03 us
    psum x1 -> x0, waiting for transfers between devices: 60.8 us -> none  [shards(): grad_kernel = lax.psum(jnp.sum(d_hidden * second, axis=0), 'dp')]
    ppermute x0 -> x1, waiting for transfers between devices: none -> 60.6 us  [shards(): other = lax.ppermute(partial, 'dp', perm=[(0, 1), (1, 0)])]
    all_to_all x4 -> x2, waiting for transfers between devices: 54 us -> 33.6 us  [the longest x1 28 us: shards(): lax.all_to_all(spread(both), 'seq', split_axis=2, concat_axis=1, tiled=True)]
    all_to_all x4 -> x2, starting transfers between devices: 36 us -> 21.3 us  [the longest x1 13.8 us: shards(): lax.all_to_all(spread(both), 'seq', split_axis=2, concat_axis=1, tiled=True)]
    ppermute x0 -> x1, starting transfers between devices: none -> 4.3 us  [shards(): other = lax.ppermute(partial, 'dp', perm=[(0, 1), (1, 0)])]
    unnamed x33 -> x19, local copies, waits for them, and re-layouts: 11.8 us -> 8.79 us
    convert_element_type x2 -> x1, local copies, waits for them, and re-layouts: 4 us -> 3.71 us  [unmix_columns(): return jnp.einsum('cqr,sqcd->srcd', second_blocks, scaled, preferred_elem...]
  transfers between devices with their start and end apart: 5 -> 3, of which waited for: 5 -> 3; matrix products, arithmetic and copies ran while one was open for 9% -> 3% of each run, Pallas kernels for 0% -> 0%
where the time goes in v1:
time: 145 us; the launch traced here: 144 us
  waiting for transfers between devices  94.2 us (65%)
  starting transfers between devices  25.6 us (18%)
  local copies, waits for them, and re-layouts  18.8 us (13%)
  matrix products  3.03 us (2%)
  other arithmetic  1.7 us (1%)
    ppermute x1, waiting for transfers between devices, shards(): other = lax.ppermute(partial, 'dp', perm=[(0, 1), (1, 0)])  60.6 us
    all_to_all x1, waiting for transfers between devices, shards(): lax.all_to_all(spread(both), 'seq', split_axis=2, concat_axis=1, tiled=True)  28 us
    all_to_all x1, starting transfers between devices, shards(): lax.all_to_all(spread(both), 'seq', split_axis=2, concat_axis=1, tiled=True)  13.8 us
    unnamed x19, local copies, waits for them, and re-layouts  8.79 us
    all_to_all x1, starting transfers between devices, shards(): lax.all_to_all(unmix_columns(scaled), 'seq', split_axis=1, concat_axis=2,...  7.5 us
    all_to_all x1, waiting for transfers between devices, shards(): lax.all_to_all(unmix_columns(scaled), 'seq', split_axis=1, concat_axis=2,...  5.53 us
    ppermute x1, starting transfers between devices, shards(): other = lax.ppermute(partial, 'dp', perm=[(0, 1), (1, 0)])  4.3 us
    convert_element_type x1, local copies, waits for them, and re-layouts, unmix_columns(): return jnp.einsum('cqr,sqcd->srcd', second_blocks, scaled, preferred_elem...  3.71 us
  transfers between devices with their start and end apart: 3, of which 3 were waited for; matrix products, arithmetic and copies ran while one was open for 3% of the time, Pallas kernels for 0%

profile of v1, /device:TPU:1, one launch (start us, length us, event | category | flops | bytes accessed | tf_op | source)
XLA Modules:
  0.0 144.2 jit_solution(3607669858728714218)
XLA Ops:
  0.6 0.0 copy-start
  0.6 0.0 copy-start.3
  0.7 1.3 copy.34
  2.0 0.0 copy-start.4
  2.0 1.3 copy.35
  3.3 0.2 copy.36
  3.5 0.1 fusion.3
  3.6 0.5 fusion
  4.1 0.0 copy-start.2
  4.1 2.1 %copy.37 = bf16[2,2,256,512]{3,0,1,2:T(2,128)(2,1)} copy(bf16[2,2,256,512]{2,3,0,1:T(8,128)(2,1)S(1)} %fusion) | data formatting | bytes 2097152 | tf_op jit(solution)/shard_map/convert_element_type | solution.py:16
  6.2 13.8 %all-to-all-start = ((bf16[2,2,256,512]{3,0,1,2:T(2,128)(2,1)}), bf16[2,2,256,512]{3,0,1,2:T(2,128)(2,1)S(1)}, u32[]{:S(2)}, u32[]{:S(2)}) async-start(bf16[2,2,256,512]{3,0,1,2:T(2,128)(2,1)} %copy.37), calls=%async_computation | async-start | bytes 2097152 | tf_op jit(solution)/shard_map/all_to_all | solution.py:33
  20.1 1.3 copy.41
  21.4 28.0 %all-to-all-done = bf16[2,2,256,512]{3,0,1,2:T(2,128)(2,1)S(1)} async-done(((bf16[2,2,256,512]{3,0,1,2:T(2,128)(2,1)}), bf16[2,2,256,512]{3,0,1,2:T(2,128)(2,1)S(1)}, u32[]{:S(2)}, u32[]{:S(2)}) %all-to-all-start) | async-done | bytes 1048608 | tf_op jit(solution)/shard_map/all_to_all | solution.py:33
  49.5 0.8 copy.39
  50.3 0.6 convolution_bitcast_fusion.1
  50.8 0.6 copy-done.1
  51.5 1.5 %fusion.1 = bf16[2,256,2,512]{1,3,0,2:T(8,128)(2,1)} fusion(f32[2,256,2,512]{1,3,0,2:T(8,128)S(1)} %convolution_bitcast_fusion.1, f32[256,2,512]{0,2,1:T(8,128)S(1)} %copy-done.1, bf16[2,256,256]{2,1,0:T(8,128)(2,1)S(1)} %copy-done), kind=kOutput, calls=%fused_computation.6 | convolution fusion | flops 270008320 | bytes 4456448 | tf_op jit(solution)/shard_map/cqr,sqcd->srcd/dot_general | solution.py:24
  53.0 3.7 %copy.42 = bf16[2,256,2,512]{3,0,2,1:T(2,128)(2,1)} copy(bf16[2,256,2,512]{1,3,0,2:T(8,128)(2,1)} %fusion.1) | data formatting | bytes 2097152 | tf_op jit(solution)/shard_map/convert_element_type | solution.py:26
  56.7 7.5 %all-to-all-start.1 = ((bf16[2,256,2,512]{3,0,2,1:T(2,128)(2,1)}), bf16[2,256,2,512]{3,0,2,1:T(2,128)(2,1)}, u32[]{:S(2)}, u32[]{:S(2)}) async-start(bf16[2,256,2,512]{3,0,2,1:T(2,128)(2,1)} %copy.42), calls=%async_computation.1 | async-start | bytes 2097152 | tf_op jit(solution)/shard_map/all_to_all | solution.py:41
  64.2 0.1 fusion.5
  64.3 4.3 %collective-permute-start = (f32[256,2,512]{0,2,1:T(8,128)S(1)}, f32[256,2,512]{0,2,1:T(8,128)S(1)}, u32[]{:S(2)}, u32[]{:S(2)}) collective-permute-start(f32[256,2,512]{0,2,1:T(8,128)S(1)} %fusion.5), channel_id=1, source_target_pairs={{0,1},{1,0},{2,3},{3,2},{4,5},{5,4},{6,7},{7,6},{8,9},{9,8},{10,11... | collective-permute-start | bytes 3145736 | tf_op jit(solution)/shard_map/ppermute | solution.py:38
  68.6 60.6 %collective-permute-done = f32[256,2,512]{0,2,1:T(8,128)S(1)} collective-permute-done((f32[256,2,512]{0,2,1:T(8,128)S(1)}, f32[256,2,512]{0,2,1:T(8,128)S(1)}, u32[]{:S(2)}, u32[]{:S(2)}) %collective-permute-start) | collective-permute-done | bytes 1048608 | tf_op jit(solution)/shard_map/ppermute | solution.py:38
  129.2 1.2 fusion.17
  130.4 2.3 %copy.49 = f32[256,2,512]{2,1,0:T(2,128)} copy(f32[256,2,512]{0,2,1:T(8,128)} %fusion.17) | data formatting | bytes 2097152
  132.7 5.5 %all-to-all-done.1 = bf16[2,256,2,512]{3,0,2,1:T(2,128)(2,1)} async-done(((bf16[2,256,2,512]{3,0,2,1:T(2,128)(2,1)}), bf16[2,256,2,512]{3,0,2,1:T(2,128)(2,1)}, u32[]{:S(2)}, u32[]{:S(2)}) %all-to-all-start.1) | async-done | bytes 1048608 | tf_op jit(solution)/shard_map/all_to_all | solution.py:41
  138.3 2.0 %copy.44 = bf16[2,2,128,2,512]{4,1,3,2,0:T(2,128)(2,1)S(1)} copy(bf16[2,2,128,2,512]{4,0,3,1,2:T(2,128)(2,1)} %bitcast.13) | data formatting | bytes 2097152 | tf_op jit(solution)/shard_map/all_to_all | solution.py:41
  140.3 0.6 convolution_bitcast_fusion
  140.9 0.2 fusion.2
  141.1 0.1 slice.28
  141.2 1.0 copy.46
  142.2 1.0 copy.48
  143.2 1.0 copy.47
  (7 shorter events, 0.0 us)
Async XLA Ops:
  0.6 49.7 %copy-start = (bf16[2,256,256]{2,1,0:T(8,128)(2,1)S(1)}, bf16[2,256,256]{2,1,0:T(8,128)(2,1)}, u32[]{:S(2)}) copy-start(bf16[2,256,256]{2,1,0:T(8,128)(2,1)} %param.10) | copy-start | bytes 786436
  0.6 2.6 %copy-start.3 = (bf16[1,2,256,512]{3,2,1,0:T(8,128)(2,1)S(1)}, bf16[1,2,256,512]{3,2,1,0:T(8,128)(2,1)}, u32[]{:S(2)}) copy-start(bf16[1,2,256,512]{3,2,1,0:T(8,128)(2,1)} %param.6) | copy-start | bytes 1572868
  2.0 1.7 %copy-start.4 = (bf16[2,256,256]{2,1,0:T(8,128)(2,1)S(1)}, bf16[2,256,256]{2,1,0:T(8,128)(2,1)}, u32[]{:S(2)}) copy-start(bf16[2,256,256]{2,1,0:T(8,128)(2,1)} %param.9) | copy-start | bytes 786436
  4.1 16.0 %copy-start.2 = (bf16[256,2,512]{2,1,0:T(2,128)(2,1)S(1)}, bf16[256,2,512]{2,1,0:T(2,128)(2,1)}, u32[]{:S(2)}) copy-start(bf16[256,2,512]{2,1,0:T(2,128)(2,1)} %param.8) | copy-start | bytes 1572868
  6.2 43.2 %all-to-all-start = ((bf16[2,2,256,512]{3,0,1,2:T(2,128)(2,1)}), bf16[2,2,256,512]{3,0,1,2:T(2,128)(2,1)S(1)}, u32[]{:S(2)}, u32[]{:S(2)}) async-start(bf16[2,2,256,512]{3,0,1,2:T(2,128)(2,1)} %copy.37), calls=%async_computation | async-start | bytes 2097152 | tf_op jit(solution)/shard_map/all_to_all | solution.py:33
  50.3 1.2 copy-start.1
  56.7 81.6 %all-to-all-start.1 = ((bf16[2,256,2,512]{3,0,2,1:T(2,128)(2,1)}), bf16[2,256,2,512]{3,0,2,1:T(2,128)(2,1)}, u32[]{:S(2)}, u32[]{:S(2)}) async-start(bf16[2,256,2,512]{3,0,2,1:T(2,128)(2,1)} %copy.42), calls=%async_computation.1 | async-start | bytes 2097152 | tf_op jit(solution)/shard_map/all_to_all | solution.py:41
  64.3 64.9 %collective-permute-start = (f32[256,2,512]{0,2,1:T(8,128)S(1)}, f32[256,2,512]{0,2,1:T(8,128)S(1)}, u32[]{:S(2)}, u32[]{:S(2)}) collective-permute-start(f32[256,2,512]{0,2,1:T(8,128)S(1)} %fusion.5), channel_id=1, source_target_pairs={{0,1},{1,0},{2,3},{3,2},{4,5},{5,4},{6,7},{7,6},{8,9},{9,8},{10,11... | collective-permute-start | bytes 3145736 | tf_op jit(solution)/shard_map/ppermute | solution.py:38
  130.4 9.9 %copy-start.5 = (bf16[2,256,256]{2,1,0:T(8,128)(2,1)S(1)}, bf16[2,256,256]{2,1,0:T(8,128)(2,1)}, u32[]{:S(2)}) copy-start(bf16[2,256,256]{2,1,0:T(8,128)(2,1)} %param.9) | copy-start | bytes 786436

commit v2 on v1

--- a/solution.py
+++ b/solution.py
@@ -4,7 +4,7 @@
 from jax.sharding import PartitionSpec as P
 
 
-def shards(inputs, gate, kernel, first_blocks, second_blocks, cotangent):
+def layer(inputs, gate, kernel, first_blocks, second_blocks, cotangent):
     f32 = jnp.float32
     bf16 = jnp.bfloat16
     seqs = inputs.shape[0]
@@ -37,9 +37,9 @@
     partial = jnp.sum(d_hidden * second, axis=0)
     other = lax.ppermute(partial, "dp", perm=[(0, 1), (1, 0)])
     scaled = (mixed_both * kernel).astype(bf16)
-    out_both = finish_rows(
-        lax.all_to_all(unmix_columns(scaled), "seq", split_axis=1, concat_axis=2, tiled=True)
-    )
+    unmixed = unmix_columns(scaled)
+    gathered = lax.all_to_all(unmixed, "seq", split_axis=1, concat_axis=2, tiled=True)
+    out_both = finish_rows(gathered)
     result = out_both[:seqs]
     d_inputs = out_both[seqs:]
     mixed = (result * gate32).astype(bf16)
@@ -59,7 +59,7 @@
         P("dp", "seq", None, None),
     )
     return jax.shard_map(
-        shards,
+        layer,
         mesh=mesh,
         in_specs=placed,
         out_specs=(

time: 145 us -> 145 us (level)
  no operation moved by 1% of the time
where the time goes in v2:
time: 145 us; the launch traced here: 144 us
  waiting for transfers between devices  94.2 us (65%)
  starting transfers between devices  25.6 us (18%)
  local copies, waits for them, and re-layouts  18.8 us (13%)
  matrix products  3.03 us (2%)
  other arithmetic  1.7 us (1%)
    ppermute x1, waiting for transfers between devices, layer(): other = lax.ppermute(partial, 'dp', perm=[(0, 1), (1, 0)])  60.6 us
    all_to_all x1, waiting for transfers between devices, layer(): lax.all_to_all(spread(both), 'seq', split_axis=2, concat_axis=1, tiled=True)  28 us
    all_to_all x1, starting transfers between devices, layer(): lax.all_to_all(spread(both), 'seq', split_axis=2, concat_axis=1, tiled=True)  13.8 us
    unnamed x19, local copies, waits for them, and re-layouts  8.79 us
    all_to_all x1, starting transfers between devices, layer(): lax.all_to_all(unmixed, 'seq', split_axis=1, concat_axis=2, tiled=True)  7.5 us
    all_to_all x1, waiting for transfers between devices, layer(): lax.all_to_all(unmixed, 'seq', split_axis=1, concat_axis=2, tiled=True)  5.53 us
    ppermute x1, starting transfers between devices, layer(): other = lax.ppermute(partial, 'dp', perm=[(0, 1), (1, 0)])  4.3 us
    convert_element_type x1, local copies, waits for them, and re-layouts, unmix_columns(): return jnp.einsum('cqr,sqcd->srcd', second_blocks, scaled, preferred_elem...  3.71 us
  transfers between devices with their start and end apart: 3, of which 3 were waited for; matrix products, arithmetic and copies ran while one was open for 3% of the time, Pallas kernels for 0%

profile of v2, /device:TPU:1, one launch (start us, length us, event | category | flops | bytes accessed | tf_op | source)
XLA Modules:
  0.0 144.2 jit_solution(3607669858728714218)
XLA Ops:
  0.6 0.0 copy-start
  0.7 1.3 copy.34
  2.0 0.0 copy-start.4
  2.0 1.3 copy.35
  3.3 0.2 copy.36
  3.5 0.1 fusion.3
  3.6 0.5 fusion
  4.1 0.0 copy-start.2
  4.1 2.1 %copy.37 = bf16[2,2,256,512]{3,0,1,2:T(2,128)(2,1)} copy(bf16[2,2,256,512]{2,3,0,1:T(8,128)(2,1)S(1)} %fusion) | data formatting | bytes 2097152 | tf_op jit(solution)/shard_map/convert_element_type | solution.py:16
  6.2 13.8 %all-to-all-start = ((bf16[2,2,256,512]{3,0,1,2:T(2,128)(2,1)}), bf16[2,2,256,512]{3,0,1,2:T(2,128)(2,1)S(1)}, u32[]{:S(2)}, u32[]{:S(2)}) async-start(bf16[2,2,256,512]{3,0,1,2:T(2,128)(2,1)} %copy.37), calls=%async_computation | async-start | bytes 2097152 | tf_op jit(solution)/shard_map/all_to_all | solution.py:33
  20.1 1.3 copy.41
  21.4 28.0 %all-to-all-done = bf16[2,2,256,512]{3,0,1,2:T(2,128)(2,1)S(1)} async-done(((bf16[2,2,256,512]{3,0,1,2:T(2,128)(2,1)}), bf16[2,2,256,512]{3,0,1,2:T(2,128)(2,1)S(1)}, u32[]{:S(2)}, u32[]{:S(2)}) %all-to-all-start) | async-done | bytes 1048608 | tf_op jit(solution)/shard_map/all_to_all | solution.py:33
  49.5 0.8 copy.39
  50.3 0.6 convolution_bitcast_fusion.1
  50.8 0.6 copy-done.1
  51.5 1.5 %fusion.1 = bf16[2,256,2,512]{1,3,0,2:T(8,128)(2,1)} fusion(f32[2,256,2,512]{1,3,0,2:T(8,128)S(1)} %convolution_bitcast_fusion.1, f32[256,2,512]{0,2,1:T(8,128)S(1)} %copy-done.1, bf16[2,256,256]{2,1,0:T(8,128)(2,1)S(1)} %copy-done), kind=kOutput, calls=%fused_computation.6 | convolution fusion | flops 270008320 | bytes 4456448 | tf_op jit(solution)/shard_map/cqr,sqcd->srcd/dot_general | solution.py:24
  53.0 3.7 %copy.42 = bf16[2,256,2,512]{3,0,2,1:T(2,128)(2,1)} copy(bf16[2,256,2,512]{1,3,0,2:T(8,128)(2,1)} %fusion.1) | data formatting | bytes 2097152 | tf_op jit(solution)/shard_map/convert_element_type | solution.py:26
  56.7 7.5 %all-to-all-start.1 = ((bf16[2,256,2,512]{3,0,2,1:T(2,128)(2,1)}), bf16[2,256,2,512]{3,0,2,1:T(2,128)(2,1)}, u32[]{:S(2)}, u32[]{:S(2)}) async-start(bf16[2,256,2,512]{3,0,2,1:T(2,128)(2,1)} %copy.42), calls=%async_computation.1 | async-start | bytes 2097152 | tf_op jit(solution)/shard_map/all_to_all | solution.py:41
  64.2 0.1 fusion.5
  64.3 4.3 %collective-permute-start = (f32[256,2,512]{0,2,1:T(8,128)S(1)}, f32[256,2,512]{0,2,1:T(8,128)S(1)}, u32[]{:S(2)}, u32[]{:S(2)}) collective-permute-start(f32[256,2,512]{0,2,1:T(8,128)S(1)} %fusion.5), channel_id=1, source_target_pairs={{0,1},{1,0},{2,3},{3,2},{4,5},{5,4},{6,7},{7,6},{8,9},{9,8},{10,11... | collective-permute-start | bytes 3145736 | tf_op jit(solution)/shard_map/ppermute | solution.py:38
  68.6 60.6 %collective-permute-done = f32[256,2,512]{0,2,1:T(8,128)S(1)} collective-permute-done((f32[256,2,512]{0,2,1:T(8,128)S(1)}, f32[256,2,512]{0,2,1:T(8,128)S(1)}, u32[]{:S(2)}, u32[]{:S(2)}) %collective-permute-start) | collective-permute-done | bytes 1048608 | tf_op jit(solution)/shard_map/ppermute | solution.py:38
  129.2 1.2 fusion.17
  130.4 2.3 %copy.49 = f32[256,2,512]{2,1,0:T(2,128)} copy(f32[256,2,512]{0,2,1:T(8,128)} %fusion.17) | data formatting | bytes 2097152
  132.7 5.5 %all-to-all-done.1 = bf16[2,256,2,512]{3,0,2,1:T(2,128)(2,1)} async-done(((bf16[2,256,2,512]{3,0,2,1:T(2,128)(2,1)}), bf16[2,256,2,512]{3,0,2,1:T(2,128)(2,1)}, u32[]{:S(2)}, u32[]{:S(2)}) %all-to-all-start.1) | async-done | bytes 1048608 | tf_op jit(solution)/shard_map/all_to_all | solution.py:41
  138.3 2.0 %copy.44 = bf16[2,2,128,2,512]{4,1,3,2,0:T(2,128)(2,1)S(1)} copy(bf16[2,2,128,2,512]{4,0,3,1,2:T(2,128)(2,1)} %bitcast.13) | data formatting | bytes 2097152 | tf_op jit(solution)/shard_map/all_to_all | solution.py:41
  140.3 0.0 copy-done.5
  140.3 0.6 convolution_bitcast_fusion
  140.9 0.2 fusion.2
  141.1 0.1 slice.28
  141.2 1.0 copy.46
  142.2 1.0 copy.48
  143.2 1.0 copy.47
  (7 shorter events, 0.0 us)
Async XLA Ops:
  0.6 49.7 %copy-start = (bf16[2,256,256]{2,1,0:T(8,128)(2,1)S(1)}, bf16[2,256,256]{2,1,0:T(8,128)(2,1)}, u32[]{:S(2)}) copy-start(bf16[2,256,256]{2,1,0:T(8,128)(2,1)} %param.10) | copy-start | bytes 786436
  0.6 2.6 %copy-start.3 = (bf16[1,2,256,512]{3,2,1,0:T(8,128)(2,1)S(1)}, bf16[1,2,256,512]{3,2,1,0:T(8,128)(2,1)}, u32[]{:S(2)}) copy-start(bf16[1,2,256,512]{3,2,1,0:T(8,128)(2,1)} %param.6) | copy-start | bytes 1572868
  2.0 1.7 %copy-start.4 = (bf16[2,256,256]{2,1,0:T(8,128)(2,1)S(1)}, bf16[2,256,256]{2,1,0:T(8,128)(2,1)}, u32[]{:S(2)}) copy-start(bf16[2,256,256]{2,1,0:T(8,128)(2,1)} %param.9) | copy-start | bytes 786436
  4.1 16.0 %copy-start.2 = (bf16[256,2,512]{2,1,0:T(2,128)(2,1)S(1)}, bf16[256,2,512]{2,1,0:T(2,128)(2,1)}, u32[]{:S(2)}) copy-start(bf16[256,2,512]{2,1,0:T(2,128)(2,1)} %param.8) | copy-start | bytes 1572868
  6.2 43.2 %all-to-all-start = ((bf16[2,2,256,512]{3,0,1,2:T(2,128)(2,1)}), bf16[2,2,256,512]{3,0,1,2:T(2,128)(2,1)S(1)}, u32[]{:S(2)}, u32[]{:S(2)}) async-start(bf16[2,2,256,512]{3,0,1,2:T(2,128)(2,1)} %copy.37), calls=%async_computation | async-start | bytes 2097152 | tf_op jit(solution)/shard_map/all_to_all | solution.py:33
  50.3 1.2 copy-start.1
  56.7 81.6 %all-to-all-start.1 = ((bf16[2,256,2,512]{3,0,2,1:T(2,128)(2,1)}), bf16[2,256,2,512]{3,0,2,1:T(2,128)(2,1)}, u32[]{:S(2)}, u32[]{:S(2)}) async-start(bf16[2,256,2,512]{3,0,2,1:T(2,128)(2,1)} %copy.42), calls=%async_computation.1 | async-start | bytes 2097152 | tf_op jit(solution)/shard_map/all_to_all | solution.py:41
  64.3 64.9 %collective-permute-start = (f32[256,2,512]{0,2,1:T(8,128)S(1)}, f32[256,2,512]{0,2,1:T(8,128)S(1)}, u32[]{:S(2)}, u32[]{:S(2)}) collective-permute-start(f32[256,2,512]{0,2,1:T(8,128)S(1)} %fusion.5), channel_id=1, source_target_pairs={{0,1},{1,0},{2,3},{3,2},{4,5},{5,4},{6,7},{7,6},{8,9},{9,8},{10,11... | collective-permute-start | bytes 3145736 | tf_op jit(solution)/shard_map/ppermute | solution.py:38
  130.4 9.9 %copy-start.5 = (bf16[2,256,256]{2,1,0:T(8,128)(2,1)S(1)}, bf16[2,256,256]{2,1,0:T(8,128)(2,1)}, u32[]{:S(2)}) copy-start(bf16[2,256,256]{2,1,0:T(8,128)(2,1)} %param.9) | copy-start | bytes 786436

commit v3 on v2

v3 whole, which is shorter than its diff:
```python
import jax
import jax.numpy as jnp
from jax import lax
from jax.sharding import PartitionSpec as P


def layer(inputs, gate, kernel, first_blocks, second_blocks, cotangent):
    f32 = jnp.float32
    bf16 = jnp.bfloat16
    n_seq = lax.axis_size("seq")
    n_dp = lax.axis_size("dp")
    col = lax.axis_index("dp")
    cols = second_blocks.shape[0]
    rows = first_blocks.shape[0]
    width = first_blocks.shape[1]
    gate32 = gate[0].astype(f32)
    cot = cotangent[0].astype(f32)
    d_result = (cot * gate32).astype(bf16)

    blk1 = first_blocks.reshape(rows, n_seq, cols, width)
    blk1 = jnp.swapaxes(blk1, 1, 2).reshape(rows, n_seq * cols, width)
    blk2 = lax.dynamic_index_in_dim(second_blocks, col, axis=0, keepdims=False)
    kern = lax.dynamic_index_in_dim(kernel, col, axis=1, keepdims=False).astype(f32)

    both = jnp.stack([inputs[0], d_result], axis=0)
    first = jnp.einsum("rij,trjd->trid", blk1, both, preferred_element_type=f32).astype(bf16)
    cols_in = lax.all_to_all(first, ("dp", "seq"), split_axis=2, concat_axis=1, tiled=True)
    cols_in = cols_in.reshape(2, n_dp, n_seq * rows, -1)
    mixed_both = jnp.einsum("qr,tsrd->tsqd", blk2, cols_in, preferred_element_type=f32)
    second = mixed_both[0]
    d_hidden = mixed_both[1]
    own = jnp.sum(d_hidden * second, axis=0)
    other = lax.ppermute(own, "dp", perm=[(0, 1), (1, 0)])
    scaled = (mixed_both * kern).astype(bf16)
    unmixed = jnp.einsum("qr,tsqd->tsrd", blk2, scaled, preferred_element_type=f32).astype(bf16)
    unmixed = unmixed.reshape(2, n_dp, n_seq, rows, -1)
    unmixed = jnp.transpose(unmixed, (0, 3, 1, 2, 4)).reshape(2, rows, n_dp * n_seq, -1)
    gathered = lax.all_to_all(unmixed, ("dp", "seq"), split_axis=2, concat_axis=2, tiled=True)
    out_both = jnp.einsum("rij,trid->trjd", blk1, gathered, preferred_element_type=f32)
    result = out_both[0]
    mixed = (result * gate32).astype(bf16)[None]
    grad_gate = (cot * result).astype(bf16)[None]
    grad_inputs = out_both[1].astype(bf16)[None]
    pair = jnp.where(col == 0, jnp.stack([own, other], axis=1), jnp.stack([other, own], axis=1))
    return (mixed, grad_inputs, grad_gate, pair)


def solution(mesh):
    placed = (
        P("dp", "seq", None, None),
        P("dp", "seq", None, None),
        P(None, "seq", None),
        P("seq", None, None),
        P("seq", None, None),
        P("dp", "seq", None, None),
    )
    return jax.shard_map(
        layer,
        mesh=mesh,
        in_specs=placed,
        out_specs=(
            P("dp", "seq", None, None),
            P("dp", "seq", None, None),
            P("dp", "seq", None, None),
            P(None, "seq", None),
        ),
        check_vma=False,
    )
```

time: 145 us -> 130 us (0.90)
  waiting for transfers between devices: 94.2 us -> 70.2 us
  matrix products: 3.03 us -> 7.57 us
  starting transfers between devices: 25.6 us -> 29.3 us
  local copies, waits for them, and re-layouts: 18.8 us -> 20.7 us
    ppermute x1, waiting for transfers between devices: 60.6 us -> 40.8 us  [layer(): other = lax.ppermute(own, 'dp', perm=[(0, 1), (1, 0)])]
    dot_general x4, matrix products: 3.03 us -> 7.57 us  [the longest x1 2.44 us: layer(): jnp.einsum('qr,tsqd->tsrd', blk2, scaled, preferred_element_type=f32)]
    all_to_all x2, waiting for transfers between devices: 33.6 us -> 29.3 us  [the longest x1 29.3 us: layer(): lax.all_to_all(first, ('dp', 'seq'), split_axis=2, concat_axis=1, tiled=T...]
    convert_element_type x3 -> x2, local copies, waits for them, and re-layouts: 7.14 us -> 3.1 us  [the longest x1 2.1 us: layer(): jnp.einsum('rij,trjd->trid', blk1, both, preferred_element_type=f32)]
    transpose x0 -> x2, local copies, waits for them, and re-layouts: none -> 3.85 us  [the longest x1 3.82 us: layer(): jnp.transpose(unmixed, (0, 3, 1, 2, 4)).reshape(2, rows, n_dp * n_seq, -1)]
    reshape x0 -> x2, local copies, waits for them, and re-layouts: none -> 3.42 us  [the longest x1 2.26 us: layer(): unmixed = unmixed.reshape(2, n_dp, n_seq, rows, -1)]
    all_to_all x2 -> x0, local copies, waits for them, and re-layouts: 2.84 us -> none  [the longest x1 2.03 us: layer(): lax.all_to_all(unmixed, 'seq', split_axis=1, concat_axis=2, tiled=True)]
    ppermute x1, starting transfers between devices: 4.3 us -> 6.2 us  [layer(): other = lax.ppermute(own, 'dp', perm=[(0, 1), (1, 0)])]
  transfers between devices with their start and end apart: 3 -> 3, of which waited for: 3 -> 2; matrix products, arithmetic and copies ran while one was open for 3% -> 4% of each run, Pallas kernels for 0% -> 0%
where the time goes in v3:
time: 130 us
  waiting for transfers between devices  70.2 us (54%)
  starting transfers between devices  29.3 us (23%)
  local copies, waits for them, and re-layouts  20.7 us (16%)
  matrix products  7.57 us (6%)
  other arithmetic  1.42 us (1%)
    ppermute x1, waiting for transfers between devices, layer(): other = lax.ppermute(own, 'dp', perm=[(0, 1), (1, 0)])  40.8 us
    all_to_all x1, waiting for transfers between devices, layer(): lax.all_to_all(first, ('dp', 'seq'), split_axis=2, concat_axis=1, tiled=T...  29.3 us
    all_to_all x1, starting transfers between devices, layer(): lax.all_to_all(first, ('dp', 'seq'), split_axis=2, concat_axis=1, tiled=T...  15.6 us
    unnamed x21, local copies, waits for them, and re-layouts  8.24 us
    all_to_all x1, starting transfers between devices, layer(): lax.all_to_all(unmixed, ('dp', 'seq'), split_axis=2, concat_axis=2, tiled...  7.5 us
    ppermute x1, starting transfers between devices, layer(): other = lax.ppermute(own, 'dp', perm=[(0, 1), (1, 0)])  6.2 us
    transpose x1, local copies, waits for them, and re-layouts, layer(): jnp.transpose(unmixed, (0, 3, 1, 2, 4)).reshape(2, rows, n_dp * n_seq, -1)  3.82 us
  transfers between devices with their start and end apart: 3, of which 2 were waited for; matrix products, arithmetic and copies ran while one was open for 4% of the time, Pallas kernels for 0%

profile of v3, /device:TPU:1, one launch (start us, length us, event | category | flops | bytes accessed | tf_op | source)
XLA Modules:
  0.0 130.0 jit_solution(7269356639605622888)
XLA Ops:
  0.6 0.0 copy-start
  0.7 1.2 reshape.32
  1.9 1.2 copy.37
  3.1 0.2 copy.36
  3.4 0.0 copy-start.1
  3.4 1.0 copy.38
  4.4 0.1 fusion.3
  4.5 1.5 %fusion = bf16[2,2,256,512]{2,3,0,1:T(8,128)(2,1)S(1)} fusion(bf16[2,256,256,1]{2,1,3,0:T(8,128)(2,1)S(1)} %bitcast.49, bf16[1,2,256,512]{2,3,0,1:T(8,128)(2,1)S(1)} %fusion.3, bf16[1,2,256,512]{2,3,0,1:T(8,128)(2,1)} %copy.38), kind=kOutput, calls=%fused_computation.5 | convolution fusion | flops 269484032 | bytes 2359296 | tf_op jit(solution)/shard_map/rij,trjd->trid/dot_general | solution.py:26
  6.0 2.1 %copy.40 = bf16[2,2,256,512]{3,0,1,2:T(2,128)(2,1)} copy(bf16[2,2,256,512]{2,3,0,1:T(8,128)(2,1)S(1)} %fusion) | data formatting | bytes 2097152 | tf_op jit(solution)/shard_map/convert_element_type | solution.py:26
  8.1 15.6 %all-to-all-start = ((bf16[2,2,256,512]{3,0,1,2:T(2,128)(2,1)}), bf16[2,2,256,512]{3,0,1,2:T(2,128)(2,1)S(1)}, u32[]{:S(2)}, u32[]{:S(2)}) async-start(bf16[2,2,256,512]{3,0,1,2:T(2,128)(2,1)} %copy.40), calls=%async_computation | async-start | bytes 2097152 | tf_op jit(solution)/shard_map/all_to_all | solution.py:27
  23.8 0.5 constant_dynamic-slice_fusion
  24.4 1.0 copy.43
  25.4 29.3 %all-to-all-done = bf16[2,2,256,512]{3,0,1,2:T(2,128)(2,1)S(1)} async-done(((bf16[2,2,256,512]{3,0,1,2:T(2,128)(2,1)}), bf16[2,2,256,512]{3,0,1,2:T(2,128)(2,1)S(1)}, u32[]{:S(2)}, u32[]{:S(2)}) %all-to-all-start) | async-done | bytes 1048608 | tf_op jit(solution)/shard_map/all_to_all | solution.py:27
  54.7 1.0 copy-done.3
  55.7 1.8 %convolution_bitcast_fusion.1 = f32[2,2,256,512]{2,3,1,0:T(8,128)S(1)} fusion(bf16[2,2,256,512]{3,0,2,1:T(2,128)(2,1)} %bitcast.44, bf16[2,256,256]{2,1,0:T(8,128)(2,1)} %param.10, s32[]{:T(128)S(6)} %select_n.14), kind=kOutput, calls=%fused_computation.2 | convolution fusion | flops 268435456 | bytes 3276804 | tf_op jit(solution)/shard_map/qr,tsrd->tsqd/dot_general | solution.py:29
  57.5 2.4 %fusion.1 = bf16[2,2,256,512]{3,2,1,0:T(8,128)(2,1)} fusion(f32[2,2,256,512]{2,3,1,0:T(8,128)S(1)} %convolution_bitcast_fusion.1, f32[256,512]{0,1:T(8,128)S(1)} %copy-done.4, bf16[2,256,256]{2,1,0:T(8,128)(2,1)} %param.10, s32[]{:T(128)S(6)} %select_n.14), kind=kOutput, calls=%fused_computation.6 | convolution fusion | flops 270008320 | bytes 3801092 | tf_op jit(solution)/shard_map/qr,tsqd->tsrd/dot_general | solution.py:35
  59.9 2.3 %reshape.35 = bf16[2,2,128,2,512]{4,3,2,1,0:T(2,128)(2,1)} reshape(bf16[2,2,256,512]{3,2,1,0:T(8,128)(2,1)} %fusion.1) | data formatting | bytes 2097152 | tf_op jit(solution)/shard_map/reshape | solution.py:36
  62.2 3.8 %copy.46 = bf16[2,2,2,128,512]{4,0,1,3,2:T(2,128)(2,1)} copy(bf16[2,2,2,128,512]{4,1,3,2,0:T(2,128)(2,1)} %bitcast.45) | data formatting | bytes 2097152 | tf_op jit(solution)/shard_map/transpose | solution.py:37
  66.0 7.5 %all-to-all-start.1 = ((bf16[2,2,256,512]{3,0,1,2:T(2,128)(2,1)}), bf16[2,2,256,512]{3,0,1,2:T(2,128)(2,1)}, u32[]{:S(2)}, u32[]{:S(2)}) async-start(bf16[2,2,256,512]{3,0,1,2:T(2,128)(2,1)} %bitcast.43), calls=%async_computation.1 | async-start | bytes 2097152 | tf_op jit(solution)/shard_map/all_to_all | solution.py:38
  73.5 0.9 fusion.5
  74.4 6.2 %collective-permute-start = (f32[256,512]{0,1:T(8,128)}, f32[256,512]{0,1:T(8,128)S(1)}, u32[]{:S(2)}, u32[]{:S(2)}) collective-permute-start(f32[256,512]{0,1:T(8,128)} %fusion.5), channel_id=1, source_target_pairs={{0,1},{1,0},{2,3},{3,2},{4,5},{5,4},{6,7},{7,6},{8,9},{9,8},{10,11... | collective-permute-start | bytes 1572872 | tf_op jit(solution)/shard_map/ppermute | solution.py:33
  80.6 1.3 copy.48
  81.9 40.8 %collective-permute-done = f32[256,512]{0,1:T(8,128)S(1)} collective-permute-done((f32[256,512]{0,1:T(8,128)}, f32[256,512]{0,1:T(8,128)S(1)}, u32[]{:S(2)}, u32[]{:S(2)}) %collective-permute-start) | collective-permute-done | bytes 524320 | tf_op jit(solution)/shard_map/ppermute | solution.py:33
  122.7 0.2 copy.49
  122.9 0.1 maximum_select_fusion
  123.0 1.8 %copy.53 = f32[256,2,512]{2,1,0:T(2,128)} copy(f32[256,2,512]{2,0,1:T(8,128)S(1)} %maximum_select_fusion) | data formatting | bytes 2097152
  124.8 1.8 %convolution_bitcast_fusion = f32[2,2,256,512]{2,3,0,1:T(8,128)S(1)} fusion(bf16[2,256,256,1]{2,1,3,0:T(8,128)(2,1)S(1)} %bitcast.50, bf16[2,2,256,512]{3,0,1,2:T(2,128)(2,1)} %all-to-all-done.1), kind=kOutput, calls=%fused_computation.1 | convolution fusion | flops 268435456 | bytes 3407872 | tf_op jit(solution)/shard_map/rij,trid->trjd/dot_general | solution.py:39
  126.7 0.2 fusion.2
  126.9 0.1 slice.28
  127.0 1.0 copy.51
  128.0 1.0 copy.52
  129.0 1.0 copy.50
  (14 shorter events, 0.1 us)
Async XLA Ops:
  0.6 23.2 %copy-start = (bf16[256,2,512]{2,1,0:T(2,128)(2,1)S(1)}, bf16[256,2,512]{2,1,0:T(2,128)(2,1)}, u32[]{:S(2)}) copy-start(bf16[256,2,512]{2,1,0:T(2,128)(2,1)} %param.8) | copy-start | bytes 1572868
  0.6 2.5 %copy-start.5 = (bf16[1,2,256,512]{3,2,1,0:T(8,128)(2,1)S(1)}, bf16[1,2,256,512]{3,2,1,0:T(8,128)(2,1)}, u32[]{:S(2)}) copy-start(bf16[1,2,256,512]{3,2,1,0:T(8,128)(2,1)} %param.11) | copy-start | bytes 1572868
  0.7 2.7 %copy-start.6 = (bf16[1,2,256,512]{3,2,1,0:T(8,128)(2,1)S(1)}, bf16[1,2,256,512]{3,2,1,0:T(8,128)(2,1)}, u32[]{:S(2)}) copy-start(bf16[1,2,256,512]{3,2,1,0:T(8,128)(2,1)} %param.6) | copy-start | bytes 1572868
  3.4 2.7 %copy-start.1 = (bf16[1,2,256,512]{2,3,0,1:T(8,128)(2,1)}, bf16[1,2,256,512]{2,3,0,1:T(8,128)(2,1)S(1)}, u32[]{:S(2)}) copy-start(bf16[1,2,256,512]{2,3,0,1:T(8,128)(2,1)S(1)} %copy.36) | copy-start | bytes 1572868
  8.1 46.6 %all-to-all-start = ((bf16[2,2,256,512]{3,0,1,2:T(2,128)(2,1)}), bf16[2,2,256,512]{3,0,1,2:T(2,128)(2,1)S(1)}, u32[]{:S(2)}, u32[]{:S(2)}) async-start(bf16[2,2,256,512]{3,0,1,2:T(2,128)(2,1)} %copy.40), calls=%async_computation | async-start | bytes 2097152 | tf_op jit(solution)/shard_map/all_to_all | solution.py:27
  54.7 1.0 copy-start.3
  55.7 1.8 %copy-start.4 = (f32[256,512]{0,1:T(8,128)S(1)}, f32[256,512]{0,1:T(8,128)}, u32[]{:S(2)}) copy-start(f32[256,512]{0,1:T(8,128)} %copy.43) | copy-start | bytes 1572868
  66.0 58.8 %all-to-all-start.1 = ((bf16[2,2,256,512]{3,0,1,2:T(2,128)(2,1)}), bf16[2,2,256,512]{3,0,1,2:T(2,128)(2,1)}, u32[]{:S(2)}, u32[]{:S(2)}) async-start(bf16[2,2,256,512]{3,0,1,2:T(2,128)(2,1)} %bitcast.43), calls=%async_computation.1 | async-start | bytes 2097152 | tf_op jit(solution)/shard_map/all_to_all | solution.py:38
  74.4 48.3 %collective-permute-start = (f32[256,512]{0,1:T(8,128)}, f32[256,512]{0,1:T(8,128)S(1)}, u32[]{:S(2)}, u32[]{:S(2)}) collective-permute-start(f32[256,512]{0,1:T(8,128)} %fusion.5), channel_id=1, source_target_pairs={{0,1},{1,0},{2,3},{3,2},{4,5},{5,4},{6,7},{7,6},{8,9},{9,8},{10,11... | collective-permute-start | bytes 1572872 | tf_op jit(solution)/shard_map/ppermute | solution.py:33
  124.8 1.9 %copy-start.2 = (bf16[1,2,256,512]{2,3,0,1:T(8,128)(2,1)S(1)}, bf16[1,2,256,512]{2,3,0,1:T(8,128)(2,1)}, u32[]{:S(2)}) copy-start(bf16[1,2,256,512]{2,3,0,1:T(8,128)(2,1)} %copy-done.1) | copy-start | bytes 1572868
